TPU v7x, 256 devices: a whole 4x4x8 slice. The times are simulated.
256 devices in a mesh: dp: 32 (over z, y), expert: 8 (over x, core).
Axes of the slice: x: 4, y: 4, z: 8, core: 2. Of those that a mesh axis runs over, the one named last changes fastest.
Arguments:
- tokens: bfloat16 [32768, 2048], P(('dp', 'expert')), may hold values from -6 to 6
- routes: int32 [32768, 2], P(('dp', 'expert')), may hold values from 0 to 127, all different within a row; in each aligned block of 128 rows (0 to 127, 128 to 255, ...) at most 4 rows name the same one
- gate_codes: int32 [32768, 2], P(('dp', 'expert')), may hold values from 1 to 1024
- w_gate: bfloat16 [256, 2048, 384], P(('dp', 'expert')), may hold values from -0.125 to 0.125
- w_up: bfloat16 [256, 2048, 384], P(('dp', 'expert')), may hold values from -0.125 to 0.125
- w_down: bfloat16 [256, 384, 2048], P(('dp', 'expert')), may hold values from -0.21875 to 0.21875
- cot: bfloat16 [32768, 2048], P(('dp', 'expert')), may hold values from -6 to 6
Outputs:
- mixed: bfloat16 [32768, 2048], P(('dp', 'expert'))
- d_tokens: bfloat16 [32768, 2048], P(('dp', 'expert'))
- d_gate: bfloat16 [256, 2048, 384], P(('dp', 'expert'))
- d_up: bfloat16 [256, 2048, 384], P(('dp', 'expert'))
- d_down: bfloat16 [256, 384, 2048], P(('dp', 'expert'))
Inputs may be any that keep to these rules, and one draw needn't show every extreme that they name: `routes`: each row names 2 different experts; among the 128 rows of one device no expert is named more than 4 times, a bound that some block reaches. `gate_codes`: the gate weight is the value divided by 1024.
All inputs are finite; a program needn't handle non-finite values.
Results may differ from a plain program's by a relative error of at most 0.012.
Values may be sent and summed in bfloat16 or wider, within the bound.
No kernel may reach another device: no remote copies, remote signals or barrier semaphores. Data moves between devices by JAX's collectives and lax.ppermute only.
A program may use at most 128 MiB of HBM per device.

v0:
```python
import jax
import jax.numpy as jnp
from jax import lax
from jax.sharding import PartitionSpec as P


def expert_work(xrows, qrows, w_gate, w_up, w_down):
    act = jnp.dot(xrows, w_gate, preferred_element_type=jnp.float32)
    upv = jnp.dot(xrows, w_up, preferred_element_type=jnp.float32)
    sig = jax.nn.sigmoid(act)
    silu = act * sig
    hidden = (silu * upv).astype(jnp.bfloat16)
    outv = jnp.dot(hidden, w_down, preferred_element_type=jnp.float32).astype(jnp.bfloat16)
    dhid = jnp.dot(qrows, w_down.T, preferred_element_type=jnp.float32)
    dact = (dhid * upv * sig * (1.0 + act * (1.0 - sig))).astype(jnp.bfloat16)
    dupv = (dhid * silu).astype(jnp.bfloat16)
    pgrad = (
        jnp.dot(dact, w_gate.T, preferred_element_type=jnp.float32)
        + jnp.dot(dupv, w_up.T, preferred_element_type=jnp.float32)
    ).astype(jnp.bfloat16)
    grad_g = jnp.dot(xrows.T, dact, preferred_element_type=jnp.float32).astype(jnp.bfloat16)
    grad_u = jnp.dot(xrows.T, dupv, preferred_element_type=jnp.float32).astype(jnp.bfloat16)
    grad_d = jnp.dot(hidden.T, qrows, preferred_element_type=jnp.float32).astype(jnp.bfloat16)
    return (outv, pgrad, grad_g, grad_u, grad_d)


def reorder(index, n_data, n_group, slots):
    device = index // slots
    within = index % slots
    return (device % n_group * n_data + device // n_group) * slots + within


def group_major(row_pair, n_data, n_group, slots):
    return row_pair.reshape(n_data, n_group, slots).transpose(1, 0, 2).reshape(-1)


def local(tokens, routes, gate_codes, w_gate, w_up, w_down, cot):
    tok_rows, top = routes.shape
    width = tokens.shape[1]
    n_data = lax.axis_size("dp")
    n_group = lax.axis_size("expert")
    devices = n_data * n_group
    experts = devices // 2
    most = max(2, 2 * tok_rows * top // experts)
    pairs = tok_rows * top
    expert_ids = routes.reshape(pairs)
    onehot = (expert_ids[:, None] == jnp.arange(experts, dtype=jnp.int32)[None, :]).astype(
        jnp.int32
    )
    before = jnp.cumsum(onehot, axis=0) - onehot
    position = jnp.sum(before * onehot, axis=1)
    gates = gate_codes.reshape(pairs).astype(jnp.float32) / 1024.0
    qpairs = (
        (gates.reshape(tok_rows, top, 1) * cot.astype(jnp.float32)[:, None, :])
        .astype(jnp.bfloat16)
        .reshape(pairs, width)
    )
    tok_pad = jnp.concatenate([tokens, jnp.zeros((1, width), jnp.bfloat16)], axis=0)
    q_pad = jnp.concatenate([qpairs, jnp.zeros((1, width), jnp.bfloat16)], axis=0)
    pair_ids = jnp.arange(pairs, dtype=jnp.int32)
    wg = w_gate[0]
    wu = w_up[0]
    wd = w_down[0]
    total = devices * most
    halves = jnp.arange(2, dtype=jnp.int32)
    targets = (2 * expert_ids[:, None] + halves[None, :]) * most + position[:, None]
    row_pair = (
        jnp.full((total,), pairs, jnp.int32).at[targets.reshape(-1)].set(jnp.repeat(pair_ids, 2))
    )
    row_pair = group_major(row_pair, n_data, n_group, most)
    row_token = jnp.where(row_pair < pairs, row_pair // top, tok_rows)
    xsend = tok_pad[row_token].reshape(n_group, n_data, most * width)
    qsend = q_pad[row_pair].reshape(n_group, n_data, most * width)
    xrecv, qrecv = (
        lax.all_to_all(
            lax.all_to_all(xsend, "dp", split_axis=1, concat_axis=1, tiled=True),
            "expert",
            split_axis=0,
            concat_axis=0,
            tiled=True,
        ),
        lax.all_to_all(
            lax.all_to_all(qsend, "dp", split_axis=1, concat_axis=1, tiled=True),
            "expert",
            split_axis=0,
            concat_axis=0,
            tiled=True,
        ),
    )
    outv, pgrad, grad_g, grad_u, grad_d = expert_work(
        xrecv.reshape(total, width), qrecv.reshape(total, width), wg, wu, wd
    )
    oback, pback = (
        lax.all_to_all(
            lax.all_to_all(
                outv.reshape(n_group, n_data, most * width),
                "dp",
                split_axis=1,
                concat_axis=1,
                tiled=True,
            ),
            "expert",
            split_axis=0,
            concat_axis=0,
            tiled=True,
        ),
        lax.all_to_all(
            lax.all_to_all(
                pgrad.reshape(n_group, n_data, most * width),
                "dp",
                split_axis=1,
                concat_axis=1,
                tiled=True,
            ),
            "expert",
            split_axis=0,
            concat_axis=0,
            tiled=True,
        ),
    )
    back_idx = reorder(targets, n_data, n_group, most)
    pair_out = jnp.sum(oback.reshape(total, width)[back_idx].astype(jnp.float32), axis=1)
    pair_grad = jnp.sum(pback.reshape(total, width)[back_idx].astype(jnp.float32), axis=1)
    mixed = jnp.sum((gates[:, None] * pair_out).reshape(tok_rows, top, width), axis=1).astype(
        jnp.bfloat16
    )
    d_tokens = jnp.sum(pair_grad.reshape(tok_rows, top, width), axis=1).astype(jnp.bfloat16)
    return (mixed, d_tokens, grad_g[None], grad_u[None], grad_d[None])


def solution(mesh):
    placed = (
        P(("dp", "expert"), None),
        P(("dp", "expert"), None),
        P(("dp", "expert"), None),
        P(("dp", "expert"), None, None),
        P(("dp", "expert"), None, None),
        P(("dp", "expert"), None, None),
        P(("dp", "expert"), None),
    )
    return jax.shard_map(
        local,
        mesh=mesh,
        in_specs=placed,
        out_specs=(
            P(("dp", "expert"), None),
            P(("dp", "expert"), None),
            P(("dp", "expert"), None, None),
            P(("dp", "expert"), None, None),
            P(("dp", "expert"), None, None),
        ),
        check_vma=False,
    )
```

profile of v0, /device:TPU:11, one launch (start us, length us, event | category | flops | bytes accessed | tf_op | source)
XLA Modules:
  0.0 744.6 jit_solution(10845163730356967747)
XLA Ops:
  0.7 0.9 copy.78
  1.7 0.1 eq.29
  2.0 0.2 fusion.18
  2.3 0.2 fusion.20
  2.5 0.1 multiply_add_fusion.1
  2.6 0.1 add.201
  2.9 2.4 scatter_custom_fusion
  5.8 6.1 gather_fusion
  11.9 7.9 %reshape.463 = bf16[8,32,8192]{2,1,0:T(8,128)(2,1)} reshape(bf16[1024,2048]{1,0:T(8,128)(2,1)} %gather_fusion) | data formatting | bytes 8388608 | tf_op jit(solution)/shard_map/reshape | solution.py:72
  19.8 6.5 copy.83
  26.2 11.3 %all-to-all-start = ((bf16[8,32,8192]{2,0,1:T(8,128)(2,1)}), bf16[8,32,8192]{2,0,1:T(8,128)(2,1)}, u32[]{:S(2)}, u32[]{:S(2)}) async-start(bf16[8,32,8192]{2,0,1:T(8,128)(2,1)} %copy.83), calls=%async_computation | async-start | bytes 8388608 | tf_op jit(solution)/shard_map/all_to_all | solution.py:76
  37.9 2.4 mul.120
  40.3 3.7 mul.121
  44.0 1.8 multiply_convert_fusion
  45.9 6.0 gather_fusion.2
  51.9 7.9 %reshape.467 = bf16[8,32,8192]{2,1,0:T(8,128)(2,1)} reshape(bf16[1024,2048]{1,0:T(8,128)(2,1)} %gather_fusion.2) | data formatting | bytes 8388608 | tf_op jit(solution)/shard_map/reshape | solution.py:73
  59.8 6.4 copy.89
  66.2 65.7 %all-to-all-done = bf16[8,32,8192]{2,0,1:T(8,128)(2,1)} async-done(((bf16[8,32,8192]{2,0,1:T(8,128)(2,1)}), bf16[8,32,8192]{2,0,1:T(8,128)(2,1)}, u32[]{:S(2)}, u32[]{:S(2)}) %all-to-all-start) | async-done | bytes 4194336 | tf_op jit(solution)/shard_map/all_to_all | solution.py:76
  132.0 18.5 %all-to-all-start.4 = ((bf16[8,32,8192]{2,0,1:T(8,128)(2,1)}), bf16[8,32,8192]{2,0,1:T(8,128)(2,1)}, u32[]{:S(2)}, u32[]{:S(2)}) async-start(bf16[8,32,8192]{2,0,1:T(8,128)(2,1)} %copy.89), calls=%async_computation.4 | async-start | bytes 8388608 | tf_op jit(solution)/shard_map/all_to_all | solution.py:83
  150.5 6.4 copy.84
  156.9 88.0 %all-to-all-done.4 = bf16[8,32,8192]{2,0,1:T(8,128)(2,1)} async-done(((bf16[8,32,8192]{2,0,1:T(8,128)(2,1)}), bf16[8,32,8192]{2,0,1:T(8,128)(2,1)}, u32[]{:S(2)}, u32[]{:S(2)}) %all-to-all-start.4) | async-done | bytes 4194336 | tf_op jit(solution)/shard_map/all_to_all | solution.py:83
  244.9 7.8 %all-to-all-start.1 = ((bf16[8,32,8192]{2,1,0:T(8,128)(2,1)}), bf16[8,32,8192]{2,1,0:T(8,128)(2,1)}, u32[]{:S(2)}, u32[]{:S(2)}) async-start(bf16[8,32,8192]{2,1,0:T(8,128)(2,1)} %copy.84), calls=%async_computation.1 | async-start | bytes 8388608 | tf_op jit(solution)/shard_map/all_to_all | solution.py:75
  252.7 6.4 copy.90
  259.1 41.4 %all-to-all-done.1 = bf16[8,32,8192]{2,1,0:T(8,128)(2,1)} async-done(((bf16[8,32,8192]{2,1,0:T(8,128)(2,1)}), bf16[8,32,8192]{2,1,0:T(8,128)(2,1)}, u32[]{:S(2)}, u32[]{:S(2)}) %all-to-all-start.1) | async-done | bytes 4194336 | tf_op jit(solution)/shard_map/all_to_all | solution.py:75
  300.6 6.4 all-to-all-start.5
  307.0 7.9 %reshape.464 = bf16[1024,2048]{1,0:T(8,128)(2,1)} reshape(bf16[8,32,8192]{2,1,0:T(8,128)(2,1)} %all-to-all-done.1) | data formatting | bytes 8388608 | tf_op jit(solution)/shard_map/reshape | solution.py:91
  314.9 6.3 fusion.7
  321.2 3.5 fusion.11
  324.7 30.2 %all-to-all-done.5 = bf16[8,32,8192]{2,1,0:T(8,128)(2,1)} async-done(((bf16[8,32,8192]{2,1,0:T(8,128)(2,1)}), bf16[8,32,8192]{2,1,0:T(8,128)(2,1)}, u32[]{:S(2)}, u32[]{:S(2)}) %all-to-all-start.5) | async-done | bytes 4194336 | tf_op jit(solution)/shard_map/all_to_all | solution.py:82
  354.8 8.0 %reshape.468 = bf16[1024,2048]{1,0:T(8,128)(2,1)} reshape(bf16[8,32,8192]{2,1,0:T(8,128)(2,1)} %all-to-all-done.5) | data formatting | bytes 8388608 | tf_op jit(solution)/shard_map/reshape | solution.py:91
  362.8 7.1 multiply_convert_fusion.1
  369.9 0.9 copy-done.12
  370.8 4.3 convolution_convert_fusion
  375.1 7.9 %reshape.465 = bf16[8,32,8192]{2,1,0:T(8,128)(2,1)} reshape(bf16[1024,2048]{1,0:T(8,128)(2,1)} %convolution_convert_fusion) | data formatting | bytes 8388608 | tf_op jit(solution)/shard_map/reshape | solution.py:96
  383.0 6.4 copy.85
  389.4 5.1 all-to-all-start.2
  394.5 3.6 fusion.9
  398.2 4.3 add_convert_fusion
  402.5 7.9 %reshape.469 = bf16[8,32,8192]{2,1,0:T(8,128)(2,1)} reshape(bf16[1024,2048]{1,0:T(8,128)(2,1)} %add_convert_fusion) | data formatting | bytes 8388608 | tf_op jit(solution)/shard_map/reshape | solution.py:109
  410.5 6.4 copy.91
  416.9 71.7 %all-to-all-done.2 = bf16[8,32,8192]{2,0,1:T(8,128)(2,1)} async-done(((bf16[8,32,8192]{2,0,1:T(8,128)(2,1)}), bf16[8,32,8192]{2,0,1:T(8,128)(2,1)}, u32[]{:S(2)}, u32[]{:S(2)}) %all-to-all-start.2) | async-done | bytes 4194336 | tf_op jit(solution)/shard_map/all_to_all | solution.py:95
  488.6 6.9 all-to-all-start.6
  495.5 6.5 copy.86
  502.0 90.9 %all-to-all-done.6 = bf16[8,32,8192]{2,0,1:T(8,128)(2,1)} async-done(((bf16[8,32,8192]{2,0,1:T(8,128)(2,1)}), bf16[8,32,8192]{2,0,1:T(8,128)(2,1)}, u32[]{:S(2)}, u32[]{:S(2)}) %all-to-all-start.6) | async-done | bytes 4194336 | tf_op jit(solution)/shard_map/all_to_all | solution.py:108
  592.9 6.0 all-to-all-start.3
  598.9 6.5 copy.92
  605.4 41.4 %all-to-all-done.3 = bf16[8,32,8192]{2,1,0:T(8,128)(2,1)} async-done(((bf16[8,32,8192]{2,1,0:T(8,128)(2,1)}), bf16[8,32,8192]{2,1,0:T(8,128)(2,1)}, u32[]{:S(2)}, u32[]{:S(2)}) %all-to-all-start.3) | async-done | bytes 4194336 | tf_op jit(solution)/shard_map/all_to_all | solution.py:94
  646.8 6.6 all-to-all-start.7
  653.3 0.3 compare_select_fusion
  653.9 5.3 fusion.2
  659.2 3.6 fusion.1
  662.8 3.6 fusion
  666.4 7.9 %reshape.466 = bf16[1024,2048]{1,0:T(8,128)(2,1)} reshape(bf16[8,32,8192]{2,1,0:T(8,128)(2,1)} %all-to-all-done.3) | data formatting | bytes 8388608 | tf_op jit(solution)/shard_map/reshape | solution.py:122
  674.3 8.0 %gather_fusion.1 = bf16[512,2048]{1,0:T(8,128)(2,1)} fusion(bf16[1024,2048]{1,0:T(8,128)(2,1)} %reshape.466, s32[1024]{0:T(1024)S(1)} %pad_clamp_fusion), kind=kCustom, calls=%fused_computation.1 | custom fusion | bytes 4196352 | tf_op jit(solution)/shard_map/gather | solution.py:122
  682.2 5.6 reshape.514
  687.9 8.5 %reduce_sum.48 = f32[256,2048]{1,0:T(8,128)} reduce(f32[256,2,2048]{2,1,0:T(2,128)} %reshape.514, f32[]{:T(128)} %constant.88.clone.1), dimensions={1}, to_apply=%region_4.5 | reduce | flops 524288 | bytes 6291460 | tf_op jit(solution)/shard_map/reduce_sum | solution.py:122
  696.4 3.5 reduce_sum.49
  699.9 5.6 multiply_reduce_fusion
  705.5 7.9 %reshape.470 = bf16[1024,2048]{1,0:T(8,128)(2,1)} reshape(bf16[8,32,8192]{2,1,0:T(8,128)(2,1)} %all-to-all-done.7) | data formatting | bytes 8388608 | tf_op jit(solution)/shard_map/reshape | solution.py:123
  713.4 8.2 %gather_fusion.3 = bf16[512,2048]{1,0:T(8,128)(2,1)} fusion(bf16[1024,2048]{1,0:T(8,128)(2,1)} %reshape.470, s32[1024]{0:T(1024)S(1)} %pad_clamp_fusion), kind=kCustom, calls=%fused_computation.3 | custom fusion | bytes 4196352 | tf_op jit(solution)/shard_map/gather | solution.py:123
  721.6 5.5 reshape.515
  727.1 8.5 %reduce_sum.51 = f32[256,2048]{1,0:T(8,128)} reduce(f32[256,2,2048]{2,1,0:T(2,128)} %reshape.515, f32[]{:T(128)} %constant.88.clone.1), dimensions={1}, to_apply=%region_6.7 | reduce | flops 524288 | bytes 6291460 | tf_op jit(solution)/shard_map/reduce_sum | solution.py:123
  735.6 3.6 reshape.471
  739.2 5.0 reduce_sum.52
  (53 shorter events, 1.4 us)
Async XLA Ops:
  0.6 362.2 %copy-start = (bf16[1,384,2048]{2,1,0:T(8,128)(2,1)S(1)}, bf16[1,384,2048]{2,1,0:T(8,128)(2,1)}, u32[]{:S(2)}) copy-start(bf16[1,384,2048]{2,1,0:T(8,128)(2,1)} %param.12) | copy-start | bytes 4718596
  0.6 5.1 copy-start.10
  26.2 11.3 %copy-start.11 = (s32[128,2]{0,1:T(2,128)S(1)}, s32[128,2]{0,1:T(2,128)}, u32[]{:S(2)}) copy-start(s32[128,2]{0,1:T(2,128)} %param.9) | copy-start | bytes 3076
  26.2 11.6 %copy-start.9 = (bf16[128,2048]{1,0:T(8,128)(2,1)S(1)}, bf16[128,2048]{1,0:T(8,128)(2,1)}, u32[]{:S(2)}) copy-start(bf16[128,2048]{1,0:T(8,128)(2,1)} %param.13) | copy-start | bytes 1572868
  26.2 105.7 %all-to-all-start = ((bf16[8,32,8192]{2,0,1:T(8,128)(2,1)}), bf16[8,32,8192]{2,0,1:T(8,128)(2,1)}, u32[]{:S(2)}, u32[]{:S(2)}) async-start(bf16[8,32,8192]{2,0,1:T(8,128)(2,1)} %copy.83), calls=%async_computation | async-start | bytes 8388608 | tf_op jit(solution)/shard_map/all_to_all | solution.py:76
  132.0 112.9 %all-to-all-start.4 = ((bf16[8,32,8192]{2,0,1:T(8,128)(2,1)}), bf16[8,32,8192]{2,0,1:T(8,128)(2,1)}, u32[]{:S(2)}, u32[]{:S(2)}) async-start(bf16[8,32,8192]{2,0,1:T(8,128)(2,1)} %copy.89), calls=%async_computation.4 | async-start | bytes 8388608 | tf_op jit(solution)/shard_map/all_to_all | solution.py:83
  244.9 55.7 %all-to-all-start.1 = ((bf16[8,32,8192]{2,1,0:T(8,128)(2,1)}), bf16[8,32,8192]{2,1,0:T(8,128)(2,1)}, u32[]{:S(2)}, u32[]{:S(2)}) async-start(bf16[8,32,8192]{2,1,0:T(8,128)(2,1)} %copy.84), calls=%async_computation.1 | async-start | bytes 8388608 | tf_op jit(solution)/shard_map/all_to_all | solution.py:75
  300.6 54.3 %all-to-all-start.5 = ((bf16[8,32,8192]{2,1,0:T(8,128)(2,1)}), bf16[8,32,8192]{2,1,0:T(8,128)(2,1)}, u32[]{:S(2)}, u32[]{:S(2)}) async-start(bf16[8,32,8192]{2,1,0:T(8,128)(2,1)} %copy.90), calls=%async_computation.5 | async-start | bytes 8388608 | tf_op jit(solution)/shard_map/all_to_all | solution.py:82
  314.9 6.3 copy-start.2
  314.9 6.3 copy-start.4
  369.9 0.9 copy-start.12
  389.4 99.1 %all-to-all-start.2 = ((bf16[8,32,8192]{2,0,1:T(8,128)(2,1)}), bf16[8,32,8192]{2,0,1:T(8,128)(2,1)}, u32[]{:S(2)}, u32[]{:S(2)}) async-start(bf16[8,32,8192]{2,0,1:T(8,128)(2,1)} %copy.85), calls=%async_computation.2 | async-start | bytes 8388608 | tf_op jit(solution)/shard_map/all_to_all | solution.py:95
  394.5 3.7 copy-start.5
  394.5 3.7 copy-start.7
  488.6 104.3 %all-to-all-start.6 = ((bf16[8,32,8192]{2,0,1:T(8,128)(2,1)}), bf16[8,32,8192]{2,0,1:T(8,128)(2,1)}, u32[]{:S(2)}, u32[]{:S(2)}) async-start(bf16[8,32,8192]{2,0,1:T(8,128)(2,1)} %copy.91), calls=%async_computation.6 | async-start | bytes 8388608 | tf_op jit(solution)/shard_map/all_to_all | solution.py:108
  592.9 53.9 %all-to-all-start.3 = ((bf16[8,32,8192]{2,1,0:T(8,128)(2,1)}), bf16[8,32,8192]{2,1,0:T(8,128)(2,1)}, u32[]{:S(2)}, u32[]{:S(2)}) async-start(bf16[8,32,8192]{2,1,0:T(8,128)(2,1)} %copy.86), calls=%async_computation.3 | async-start | bytes 8388608 | tf_op jit(solution)/shard_map/all_to_all | solution.py:94
  605.4 48.5 %copy-start.13 = (bf16[1024,384]{1,0:T(8,128)(2,1)S(1)}, bf16[1024,384]{1,0:T(8,128)(2,1)}, u32[]{:S(2)}) copy-start(bf16[1024,384]{1,0:T(8,128)(2,1)} %copy-done.12) | copy-start | bytes 2359300
  646.8 58.7 %all-to-all-start.7 = ((bf16[8,32,8192]{2,1,0:T(8,128)(2,1)}), bf16[8,32,8192]{2,1,0:T(8,128)(2,1)}, u32[]{:S(2)}, u32[]{:S(2)}) async-start(bf16[8,32,8192]{2,1,0:T(8,128)(2,1)} %copy.92), calls=%async_computation.7 | async-start | bytes 8388608 | tf_op jit(solution)/shard_map/all_to_all | solution.py:107
  653.8 5.4 copy-start.3
  653.9 5.3 copy-start.8
  659.2 3.6 copy-start.6
  735.6 8.6 %copy-start.1 = (bf16[1,384,2048]{2,1,0:T(8,128)(2,1)S(1)}, bf16[1,384,2048]{2,1,0:T(8,128)(2,1)}, u32[]{:S(2)}) copy-start(bf16[1,384,2048]{2,1,0:T(8,128)(2,1)} %param.12) | copy-start | bytes 4718596
where the time goes:
time: 756 us; the launch traced here: 745 us
  waiting for transfers between devices  429 us (57%)
  local copies, waits for them, and re-layouts  173 us (23%)
  starting transfers between devices  68.7 us (9%)
  matrix products  41.6 us (6%)
  other arithmetic  30.3 us (4%)
    all_to_all x1, waiting for transfers between devices, local(): lax.all_to_all(pgrad.reshape(n_group, n_data, most * width), 'dp', split_...  90.9 us
    all_to_all x1, waiting for transfers between devices, local(): lax.all_to_all(qsend, 'dp', split_axis=1, concat_axis=1, tiled=True)  88 us
    all_to_all x1, waiting for transfers between devices, local(): lax.all_to_all(outv.reshape(n_group, n_data, most * width), 'dp', split_a...  71.7 us
    all_to_all x1, waiting for transfers between devices, local(): lax.all_to_all(xsend, 'dp', split_axis=1, concat_axis=1, tiled=True)  65.7 us
    all_to_all x1, waiting for transfers between devices, local(): lax.all_to_all(lax.all_to_all(xsend, 'dp', split_axis=1, concat_axis=1, t...  41.4 us
    all_to_all x1, waiting for transfers between devices, local(): lax.all_to_all(lax.all_to_all(outv.reshape(n_group, n_data, most * width)...  41.4 us
    all_to_all x1, waiting for transfers between devices, local(): lax.all_to_all(lax.all_to_all(qsend, 'dp', split_axis=1, concat_axis=1, t...  30.2 us
    all_to_all x1, starting transfers between devices, local(): lax.all_to_all(qsend, 'dp', split_axis=1, concat_axis=1, tiled=True)  18.5 us
  transfers between devices with their start and end apart: 8, of which 7 were waited for; matrix products, arithmetic and copies ran while one was open for 20% of the time, Pallas kernels for 0%

commit v1 on v0

--- a/solution.py
+++ b/solution.py
@@ -2,6 +2,26 @@
 import jax.numpy as jnp
 from jax import lax
 from jax.sharding import PartitionSpec as P
+
+
+def use_counts(point, which_axis):
+    a_next = jax.lax.axis_index(which_axis)
+    base_arr = jax.lax.axis_size(which_axis)
+    p_next, opened = (base_arr, a_next)
+    ready = list(point.shape)
+    lower = point.shape[0] // p_next
+    ready[0] = lower
+    carry = ready[0]
+    ready[0] = carry * p_next
+    src_i = 0
+    r1 = jnp.zeros(ready, point.dtype)
+    while src_i < p_next:
+        plain = lax.dynamic_slice_in_dim(point, (opened ^ src_i) * lower, lower, axis=0)
+        if src_i:
+            plain = jax.lax.ppermute(plain, which_axis, [(j, j ^ src_i) for j in range(p_next)])
+        r1 = lax.dynamic_update_slice_in_dim(r1, plain, (opened ^ src_i) * carry, axis=0)
+        src_i += 1
+    return r1
 
 
 def expert_work(xrows, qrows, w_gate, w_up, w_down):
@@ -72,13 +92,7 @@
     xsend = tok_pad[row_token].reshape(n_group, n_data, most * width)
     qsend = q_pad[row_pair].reshape(n_group, n_data, most * width)
     xrecv, qrecv = (
-        lax.all_to_all(
-            lax.all_to_all(xsend, "dp", split_axis=1, concat_axis=1, tiled=True),
-            "expert",
-            split_axis=0,
-            concat_axis=0,
-            tiled=True,
-        ),
+        use_counts(lax.all_to_all(xsend, "dp", split_axis=1, concat_axis=1, tiled=True), "expert"),
         lax.all_to_all(
             lax.all_to_all(qsend, "dp", split_axis=1, concat_axis=1, tiled=True),
             "expert",

time: 756 us -> 739 us (0.978)
  waiting for transfers between devices: 429 us -> 375 us
  local copies, waits for them, and re-layouts: 173 us -> 215 us
    ppermute x0 -> x7, waiting for transfers between devices: none -> 53.6 us  [use_counts(): jax.lax.ppermute(plain, which_axis, [(j, j ^ src_i) for j in range(p_next)])]
    all_to_all x1 -> x0, waiting for transfers between devices: 41.4 us -> none  [local(): lax.all_to_all(lax.all_to_all(xsend, 'dp', split_axis=1, concat_axis=1, t...]
    all_to_all x1, waiting for transfers between devices: 41.4 us -> 0.01 us  [local(): lax.all_to_all(lax.all_to_all(outv.reshape(n_group, n_data, most * width)...]
    all_to_all x1, waiting for transfers between devices: 0.01 us -> 41.3 us  [local(): lax.all_to_all(lax.all_to_all(pgrad.reshape(n_group, n_data, most * width...]
    all_to_all x1, waiting for transfers between devices: 88 us -> 47.8 us  [local(): lax.all_to_all(qsend, 'dp', split_axis=1, concat_axis=1, tiled=True)]
    dynamic_slice x0 -> x8, local copies, waits for them, and re-layouts: none -> 32.2 us  [use_counts(): lax.dynamic_slice_in_dim(point, (opened ^ src_i) * lower, lower, axis=0)]
    all_to_all x1, waiting for transfers between devices: 30.2 us -> 0.01 us  [local(): lax.all_to_all(lax.all_to_all(qsend, 'dp', split_axis=1, concat_axis=1, t...]
    all_to_all x1, waiting for transfers between devices: 71.7 us -> 90.9 us  [local(): lax.all_to_all(outv.reshape(n_group, n_data, most * width), 'dp', split_a...]
  transfers between devices with their start and end apart: 8 -> 14, of which waited for: 7 -> 7; matrix products, arithmetic and copies ran while one was open for 20% -> 25% of each run, Pallas kernels for 0% -> 0%
where the time goes in v1:
time: 739 us; the launch traced here: 728 us
  waiting for transfers between devices  375 us (51%)
  local copies, waits for them, and re-layouts  215 us (29%)
  starting transfers between devices  67.6 us (9%)
  matrix products  38.2 us (5%)
  other arithmetic  30.5 us (4%)
    all_to_all x1, waiting for transfers between devices, local(): lax.all_to_all(outv.reshape(n_group, n_data, most * width), 'dp', split_a...  90.9 us
    all_to_all x1, waiting for transfers between devices, local(): lax.all_to_all(pgrad.reshape(n_group, n_data, most * width), 'dp', split_...  75.7 us
    all_to_all x1, waiting for transfers between devices, local(): lax.all_to_all(xsend, 'dp', split_axis=1, concat_axis=1, tiled=True)  65.6 us
    ppermute x7, waiting for transfers between devices, use_counts(): jax.lax.ppermute(plain, which_axis, [(j, j ^ src_i) for j in range(p_next)])  53.6 us
    all_to_all x1, waiting for transfers between devices, local(): lax.all_to_all(qsend, 'dp', split_axis=1, concat_axis=1, tiled=True)  47.8 us
    all_to_all x1, waiting for transfers between devices, local(): lax.all_to_all(lax.all_to_all(pgrad.reshape(n_group, n_data, most * width...  41.3 us
    dynamic_slice x8, local copies, waits for them, and re-layouts, use_counts(): lax.dynamic_slice_in_dim(point, (opened ^ src_i) * lower, lower, axis=0)  32.2 us
    ppermute x7, starting transfers between devices, use_counts(): jax.lax.ppermute(plain, which_axis, [(j, j ^ src_i) for j in range(p_next)])  19.1 us
  transfers between devices with their start and end apart: 14, of which 7 were waited for; matrix products, arithmetic and copies ran while one was open for 25% of the time, Pallas kernels for 0%

profile of v1, /device:TPU:11, one launch (start us, length us, event | category | flops | bytes accessed | tf_op | source)
XLA Modules:
  0.0 727.7 jit_solution(15128960298292120349)
XLA Ops:
  2.9 2.4 scatter_custom_fusion
  6.8 6.1 gather_fusion
  12.9 7.9 %reshape.463 = bf16[8,32,8192]{2,1,0:T(8,128)(2,1)} reshape(bf16[1024,2048]{1,0:T(8,128)(2,1)} %gather_fusion) | data formatting | bytes 8388608 | tf_op jit(solution)/shard_map/reshape | solution.py:92
  20.8 6.5 copy.104
  27.2 11.3 %all-to-all-start = ((bf16[8,32,8192]{2,0,1:T(8,128)(2,1)}), bf16[8,32,8192]{2,0,1:T(8,128)(2,1)}, u32[]{:S(2)}, u32[]{:S(2)}) async-start(bf16[8,32,8192]{2,0,1:T(8,128)(2,1)} %copy.104), calls=%async_computation | async-start | bytes 8388608 | tf_op jit(solution)/shard_map/all_to_all | solution.py:95
  38.9 2.4 mul.120
  41.3 3.7 mul.121
  45.0 1.8 multiply_convert_fusion
  46.9 6.0 gather_fusion.2
  52.9 8.0 %reshape.467 = bf16[8,32,8192]{2,1,0:T(8,128)(2,1)} reshape(bf16[1024,2048]{1,0:T(8,128)(2,1)} %gather_fusion.2) | data formatting | bytes 8388608 | tf_op jit(solution)/shard_map/reshape | solution.py:93
  60.9 6.5 copy.117
  67.3 65.6 %all-to-all-done = bf16[8,32,8192]{2,0,1:T(8,128)(2,1)} async-done(((bf16[8,32,8192]{2,0,1:T(8,128)(2,1)}), bf16[8,32,8192]{2,0,1:T(8,128)(2,1)}, u32[]{:S(2)}, u32[]{:S(2)}) %all-to-all-start) | async-done | bytes 4194336 | tf_op jit(solution)/shard_map/all_to_all | solution.py:95
  133.0 7.5 %all-to-all-start.3 = ((bf16[8,32,8192]{2,0,1:T(8,128)(2,1)}), bf16[8,32,8192]{2,0,1:T(8,128)(2,1)}, u32[]{:S(2)}, u32[]{:S(2)}) async-start(bf16[8,32,8192]{2,0,1:T(8,128)(2,1)} %copy.117), calls=%async_computation.3 | async-start | bytes 8388608 | tf_op jit(solution)/shard_map/all_to_all | solution.py:97
  140.5 22.2 %constant_dynamic-slice_fusion = (bf16[1,32,8192]{2,0,1:T(2,128)(2,1)S(1)}, bf16[1,32,8192]{2,0,1:T(2,128)(2,1)S(1)}, bf16[1,32,8192]{2,0,1:T(2,128)(2,1)S(1)}, ...) fusion(bf16[8,32,8192]{2,0,1:T(8,128)(2,1)} %all-to-all-done, ...), kind=kLoop, calls=%fused_computation.76 | loop fusion | bytes 8388640 | tf_op jit(solution)/shard_map/dynamic_slice | solution.py:19
  162.7 2.6 copy.106
  172.1 1.8 collective-permute-start.3
  175.3 12.6 %collective-permute-start.4 = (bf16[1,32,8192]{2,1,0:T(8,128)(2,1)}, bf16[1,32,8192]{2,1,0:T(8,128)(2,1)}, u32[]{:S(2)}, u32[]{:S(2)}) collective-permute-start(bf16[1,32,8192]{2,1,0:T(8,128)(2,1)} %copy.110), channel_id=1, source_target_pairs={{0,5},{1,4},{2,7},{3,6},{4,1},{5,0},{6,3},{7,2},{8,13},{9,12},{10,... | collective-permute-start | bytes 1572872 | tf_op jit(solution)/shard_map/ppermute | solution.py:21
  189.9 47.8 %all-to-all-done.3 = bf16[8,32,8192]{2,0,1:T(8,128)(2,1)} async-done(((bf16[8,32,8192]{2,0,1:T(8,128)(2,1)}), bf16[8,32,8192]{2,0,1:T(8,128)(2,1)}, u32[]{:S(2)}, u32[]{:S(2)}) %all-to-all-start.3) | async-done | bytes 4194336 | tf_op jit(solution)/shard_map/all_to_all | solution.py:97
  237.7 6.5 copy.118
  244.2 5.1 all-to-all-start.4
  249.3 2.4 broadcast_in_dim.14
  254.3 1.9 constant_dynamic-update-slice_fusion.6
  256.9 1.9 constant_dynamic-update-slice_fusion.5
  258.8 1.9 constant_dynamic-update-slice_fusion.4
  260.7 1.9 constant_dynamic-update-slice_fusion.3
  262.7 1.9 constant_dynamic-update-slice_fusion.2
  264.5 43.0 %collective-permute-done.5 = bf16[1,32,8192]{2,1,0:T(8,128)(2,1)S(1)} collective-permute-done((bf16[1,32,8192]{2,1,0:T(8,128)(2,1)S(1)}, bf16[1,32,8192]{2,1,0:T(8,128)(2,1)S(1)}, u32[]{:S(2)}, u32[]{:S(2)}) %collective-permute-start.5) | collective-permute-done | bytes 524320 | tf_op jit(solution)/shard_map/ppermute | solution.py:21
  308.5 10.6 %collective-permute-done.6 = bf16[1,32,8192]{2,1,0:T(8,128)(2,1)S(1)} collective-permute-done((bf16[1,32,8192]{2,1,0:T(8,128)(2,1)S(1)}, bf16[1,32,8192]{2,1,0:T(8,128)(2,1)S(1)}, u32[]{:S(2)}, u32[]{:S(2)}) %collective-permute-start.6) | collective-permute-done | bytes 524320 | tf_op jit(solution)/shard_map/ppermute | solution.py:21
  319.9 8.1 %reshape.464 = bf16[1024,2048]{1,0:T(8,128)(2,1)} reshape(bf16[8,32,8192]{2,1,0:T(8,128)(2,1)} %constant_dynamic-update-slice_fusion) | data formatting | bytes 8388608 | tf_op jit(solution)/shard_map/reshape | solution.py:105
  327.9 5.6 fusion.7
  333.6 8.0 %reshape.468 = bf16[1024,2048]{1,0:T(8,128)(2,1)} reshape(bf16[8,32,8192]{2,1,0:T(8,128)(2,1)} %all-to-all-done.4) | data formatting | bytes 8388608 | tf_op jit(solution)/shard_map/reshape | solution.py:105
  341.5 5.2 fusion.3
  346.7 3.9 multiply_convert_fusion.1
  350.7 2.4 fusion.9
  353.1 4.3 add_convert_fusion
  357.4 8.3 %reshape.469 = bf16[8,32,8192]{2,1,0:T(8,128)(2,1)} reshape(bf16[1024,2048]{1,0:T(8,128)(2,1)} %add_convert_fusion) | data formatting | bytes 8388608 | tf_op jit(solution)/shard_map/reshape | solution.py:123
  365.7 6.4 copy.119
  372.1 4.8 all-to-all-start.5
  376.9 4.3 convolution_convert_fusion
  381.2 7.9 %reshape.465 = bf16[8,32,8192]{2,1,0:T(8,128)(2,1)} reshape(bf16[1024,2048]{1,0:T(8,128)(2,1)} %convolution_convert_fusion) | data formatting | bytes 8388608 | tf_op jit(solution)/shard_map/reshape | solution.py:110
  389.1 6.4 copy.113
  395.6 75.7 %all-to-all-done.5 = bf16[8,32,8192]{2,0,1:T(8,128)(2,1)} async-done(((bf16[8,32,8192]{2,0,1:T(8,128)(2,1)}), bf16[8,32,8192]{2,0,1:T(8,128)(2,1)}, u32[]{:S(2)}, u32[]{:S(2)}) %all-to-all-start.5) | async-done | bytes 4194336 | tf_op jit(solution)/shard_map/all_to_all | solution.py:122
  471.2 7.0 all-to-all-start.1
  478.3 6.5 copy.120
  484.7 90.9 %all-to-all-done.1 = bf16[8,32,8192]{2,0,1:T(8,128)(2,1)} async-done(((bf16[8,32,8192]{2,0,1:T(8,128)(2,1)}), bf16[8,32,8192]{2,0,1:T(8,128)(2,1)}, u32[]{:S(2)}, u32[]{:S(2)}) %all-to-all-start.1) | async-done | bytes 4194336 | tf_op jit(solution)/shard_map/all_to_all | solution.py:109
  575.7 6.4 all-to-all-start.6
  582.1 6.5 copy.114
  588.5 41.3 %all-to-all-done.6 = bf16[8,32,8192]{2,1,0:T(8,128)(2,1)} async-done(((bf16[8,32,8192]{2,1,0:T(8,128)(2,1)}), bf16[8,32,8192]{2,1,0:T(8,128)(2,1)}, u32[]{:S(2)}, u32[]{:S(2)}) %all-to-all-start.6) | async-done | bytes 4194336 | tf_op jit(solution)/shard_map/all_to_all | solution.py:121
  629.9 6.4 all-to-all-start.2
  636.8 5.3 fusion.2
  642.1 3.6 fusion.1
  645.7 3.6 fusion
  649.3 8.0 %reshape.470 = bf16[1024,2048]{1,0:T(8,128)(2,1)} reshape(bf16[8,32,8192]{2,1,0:T(8,128)(2,1)} %all-to-all-done.6) | data formatting | bytes 8388608 | tf_op jit(solution)/shard_map/reshape | solution.py:137
  657.3 8.0 %gather_fusion.3 = bf16[512,2048]{1,0:T(8,128)(2,1)} fusion(bf16[1024,2048]{1,0:T(8,128)(2,1)} %reshape.470, s32[1024]{0:T(1024)S(1)} %pad_clamp_fusion), kind=kCustom, calls=%fused_computation.3 | custom fusion | bytes 4196352 | tf_op jit(solution)/shard_map/gather | solution.py:137
  665.2 5.7 reshape.515
  670.9 8.6 %reduce_sum.51 = f32[256,2048]{1,0:T(8,128)} reduce(f32[256,2,2048]{2,1,0:T(2,128)} %reshape.515, f32[]{:T(128)} %constant.100.clone.1), dimensions={1}, to_apply=%region_6.7 | reduce | flops 524288 | bytes 6291460 | tf_op jit(solution)/shard_map/reduce_sum | solution.py:137
  679.5 3.5 reshape.471
  683.0 5.0 reduce_sum.52
  688.0 7.9 %reshape.466 = bf16[1024,2048]{1,0:T(8,128)(2,1)} reshape(bf16[8,32,8192]{2,1,0:T(8,128)(2,1)} %all-to-all-done.2) | data formatting | bytes 8388608 | tf_op jit(solution)/shard_map/reshape | solution.py:136
  695.9 8.0 %gather_fusion.1 = bf16[512,2048]{1,0:T(8,128)(2,1)} fusion(bf16[1024,2048]{1,0:T(8,128)(2,1)} %reshape.466, s32[1024]{0:T(1024)S(1)} %pad_clamp_fusion), kind=kCustom, calls=%fused_computation.1 | custom fusion | bytes 4196352 | tf_op jit(solution)/shard_map/gather | solution.py:136
  703.8 5.7 reshape.514
  709.6 8.7 %reduce_sum.48 = f32[256,2048]{1,0:T(8,128)} reduce(f32[256,2,2048]{2,1,0:T(2,128)} %reshape.514, f32[]{:T(128)} %constant.100.clone.1), dimensions={1}, to_apply=%region_4.5 | reduce | flops 524288 | bytes 6291460 | tf_op jit(solution)/shard_map/reduce_sum | solution.py:136
  718.2 3.5 reduce_sum.49
  721.7 5.6 multiply_reduce_fusion
  (83 shorter events, 19.7 us)
Async XLA Ops:
  0.6 346.1 %copy-start = (bf16[1,2048,384]{2,1,0:T(8,128)(2,1)S(1)}, bf16[1,2048,384]{2,1,0:T(8,128)(2,1)}, u32[]{:S(2)}) copy-start(bf16[1,2048,384]{2,1,0:T(8,128)(2,1)} %param.10) | copy-start | bytes 4718596
  27.2 11.3 %copy-start.11 = (s32[128,2]{0,1:T(2,128)S(1)}, s32[128,2]{0,1:T(2,128)}, u32[]{:S(2)}) copy-start(s32[128,2]{0,1:T(2,128)} %param.9) | copy-start | bytes 3076
  27.2 11.6 %copy-start.9 = (bf16[128,2048]{1,0:T(8,128)(2,1)S(1)}, bf16[128,2048]{1,0:T(8,128)(2,1)}, u32[]{:S(2)}) copy-start(bf16[128,2048]{1,0:T(8,128)(2,1)} %param.13) | copy-start | bytes 1572868
  27.2 105.7 %all-to-all-start = ((bf16[8,32,8192]{2,0,1:T(8,128)(2,1)}), bf16[8,32,8192]{2,0,1:T(8,128)(2,1)}, u32[]{:S(2)}, u32[]{:S(2)}) async-start(bf16[8,32,8192]{2,0,1:T(8,128)(2,1)} %copy.104), calls=%async_computation | async-start | bytes 8388608 | tf_op jit(solution)/shard_map/all_to_all | solution.py:95
  133.0 104.7 %all-to-all-start.3 = ((bf16[8,32,8192]{2,0,1:T(8,128)(2,1)}), bf16[8,32,8192]{2,0,1:T(8,128)(2,1)}, u32[]{:S(2)}, u32[]{:S(2)}) async-start(bf16[8,32,8192]{2,0,1:T(8,128)(2,1)} %copy.117), calls=%async_computation.3 | async-start | bytes 8388608 | tf_op jit(solution)/shard_map/all_to_all | solution.py:97
  165.3 87.7 %collective-permute-start = (bf16[1,32,8192]{2,1,0:T(8,128)(2,1)}, bf16[1,32,8192]{2,1,0:T(8,128)(2,1)}, u32[]{:S(2)}, u32[]{:S(2)}) collective-permute-start(bf16[1,32,8192]{2,1,0:T(8,128)(2,1)} %copy.106), channel_id=1, source_target_pairs={{0,1},{1,0},{2,3},{3,2},{4,5},{5,4},{6,7},{7,6},{8,9},{9,8},{10,11... | collective-permute-start | bytes 1572872 | tf_op jit(solution)/shard_map/ppermute | solution.py:21
  167.7 88.4 %collective-permute-start.1 = (bf16[1,32,8192]{2,1,0:T(8,128)(2,1)}, bf16[1,32,8192]{2,1,0:T(8,128)(2,1)}, u32[]{:S(2)}, u32[]{:S(2)}) collective-permute-start(bf16[1,32,8192]{2,1,0:T(8,128)(2,1)} %copy.107), channel_id=1, source_target_pairs={{0,2},{1,3},{2,0},{3,1},{4,6},{5,7},{6,4},{7,5},{8,10},{9,11},{10,... | collective-permute-start | bytes 1572872 | tf_op jit(solution)/shard_map/ppermute | solution.py:21
  169.3 89.5 %collective-permute-start.2 = (bf16[1,32,8192]{2,1,0:T(8,128)(2,1)}, bf16[1,32,8192]{2,1,0:T(8,128)(2,1)}, u32[]{:S(2)}, u32[]{:S(2)}) collective-permute-start(bf16[1,32,8192]{2,1,0:T(8,128)(2,1)} %copy.108), channel_id=1, source_target_pairs={{0,3},{1,2},{2,1},{3,0},{4,7},{5,6},{6,5},{7,4},{8,11},{9,10},{10,... | collective-permute-start | bytes 1572872 | tf_op jit(solution)/shard_map/ppermute | solution.py:21
  172.1 88.6 %collective-permute-start.3 = (bf16[1,32,8192]{2,1,0:T(8,128)(2,1)}, bf16[1,32,8192]{2,1,0:T(8,128)(2,1)}, u32[]{:S(2)}, u32[]{:S(2)}) collective-permute-start(bf16[1,32,8192]{2,1,0:T(8,128)(2,1)} %copy.109), channel_id=1, source_target_pairs={{0,4},{1,5},{2,6},{3,7},{4,0},{5,1},{6,2},{7,3},{8,12},{9,13},{10,... | collective-permute-start | bytes 1572872 | tf_op jit(solution)/shard_map/ppermute | solution.py:21
  175.3 87.3 %collective-permute-start.4 = (bf16[1,32,8192]{2,1,0:T(8,128)(2,1)}, bf16[1,32,8192]{2,1,0:T(8,128)(2,1)}, u32[]{:S(2)}, u32[]{:S(2)}) collective-permute-start(bf16[1,32,8192]{2,1,0:T(8,128)(2,1)} %copy.110), channel_id=1, source_target_pairs={{0,5},{1,4},{2,7},{3,6},{4,1},{5,0},{6,3},{7,2},{8,13},{9,12},{10,... | collective-permute-start | bytes 1572872 | tf_op jit(solution)/shard_map/ppermute | solution.py:21
  244.2 89.4 %all-to-all-start.4 = ((bf16[8,32,8192]{2,1,0:T(8,128)(2,1)}), bf16[8,32,8192]{2,1,0:T(8,128)(2,1)}, u32[]{:S(2)}, u32[]{:S(2)}) async-start(bf16[8,32,8192]{2,1,0:T(8,128)(2,1)} %copy.118), calls=%async_computation.4 | async-start | bytes 8388608 | tf_op jit(solution)/shard_map/all_to_all | solution.py:96
  249.3 3.8 copy-start.10
  253.0 54.6 %collective-permute-start.5 = (bf16[1,32,8192]{2,1,0:T(8,128)(2,1)S(1)}, bf16[1,32,8192]{2,1,0:T(8,128)(2,1)S(1)}, u32[]{:S(2)}, u32[]{:S(2)}) collective-permute-start(bf16[1,32,8192]{2,1,0:T(8,128)(2,1)S(1)} %copy-done.10), channel_id=1, source_target_pairs={{0,6},{1,7},{2,4},{3,5},{4,2},{5,3},{6,0},{7,1},{8,14},{9,15},{10,... | collective-permute-start | bytes 1572872 | tf_op jit(solution)/shard_map/ppermute | solution.py:21
  256.1 62.9 %collective-permute-start.6 = (bf16[1,32,8192]{2,1,0:T(8,128)(2,1)S(1)}, bf16[1,32,8192]{2,1,0:T(8,128)(2,1)S(1)}, u32[]{:S(2)}, u32[]{:S(2)}) collective-permute-start(bf16[1,32,8192]{2,1,0:T(8,128)(2,1)S(1)} %copy.112), channel_id=1, source_target_pairs={{0,7},{1,6},{2,5},{3,4},{4,3},{5,2},{6,1},{7,0},{8,15},{9,14},{10,... | collective-permute-start | bytes 1572872 | tf_op jit(solution)/shard_map/ppermute | solution.py:21
  319.8 8.1 %copy-start.4 = (bf16[1,2048,384]{2,1,0:T(8,128)(2,1)S(1)}, bf16[1,2048,384]{2,1,0:T(8,128)(2,1)}, u32[]{:S(2)}) copy-start(bf16[1,2048,384]{2,1,0:T(8,128)(2,1)} %param.11) | copy-start | bytes 4718596
  341.5 5.2 copy-start.2
  341.5 5.2 copy-start.14
  350.7 2.4 copy-start.5
  350.7 2.4 copy-start.7
  372.1 4.8 copy-start.12
  372.1 4.8 copy-start.13
  372.1 99.2 %all-to-all-start.5 = ((bf16[8,32,8192]{2,0,1:T(8,128)(2,1)}), bf16[8,32,8192]{2,0,1:T(8,128)(2,1)}, u32[]{:S(2)}, u32[]{:S(2)}) async-start(bf16[8,32,8192]{2,0,1:T(8,128)(2,1)} %copy.119), calls=%async_computation.5 | async-start | bytes 8388608 | tf_op jit(solution)/shard_map/all_to_all | solution.py:122
  471.2 104.4 %all-to-all-start.1 = ((bf16[8,32,8192]{2,0,1:T(8,128)(2,1)}), bf16[8,32,8192]{2,0,1:T(8,128)(2,1)}, u32[]{:S(2)}, u32[]{:S(2)}) async-start(bf16[8,32,8192]{2,0,1:T(8,128)(2,1)} %copy.113), calls=%async_computation.1 | async-start | bytes 8388608 | tf_op jit(solution)/shard_map/all_to_all | solution.py:109
  575.7 54.2 %all-to-all-start.6 = ((bf16[8,32,8192]{2,1,0:T(8,128)(2,1)}), bf16[8,32,8192]{2,1,0:T(8,128)(2,1)}, u32[]{:S(2)}, u32[]{:S(2)}) async-start(bf16[8,32,8192]{2,1,0:T(8,128)(2,1)} %copy.120), calls=%async_computation.6 | async-start | bytes 8388608 | tf_op jit(solution)/shard_map/all_to_all | solution.py:121
  629.9 58.1 %all-to-all-start.2 = ((bf16[8,32,8192]{2,1,0:T(8,128)(2,1)}), bf16[8,32,8192]{2,1,0:T(8,128)(2,1)}, u32[]{:S(2)}, u32[]{:S(2)}) async-start(bf16[8,32,8192]{2,1,0:T(8,128)(2,1)} %copy.114), calls=%async_computation.2 | async-start | bytes 8388608 | tf_op jit(solution)/shard_map/all_to_all | solution.py:108
  636.8 5.3 copy-start.3
  636.8 5.3 copy-start.8
  642.1 3.6 copy-start.6
  709.6 17.7 %copy-start.1 = (bf16[1,2048,384]{2,1,0:T(8,128)(2,1)S(1)}, bf16[1,2048,384]{2,1,0:T(8,128)(2,1)}, u32[]{:S(2)}) copy-start(bf16[1,2048,384]{2,1,0:T(8,128)(2,1)} %param.10) | copy-start | bytes 4718596
